TPU v7x, 256 devices: a whole 4x4x8 slice. The times are simulated.
256 devices in a mesh: var: 8 (over y, core), tok: 32 (over x, z).
Axes of the slice: x: 4, y: 4, z: 8, core: 2. Of those that a mesh axis runs over, the one named last changes fastest.
Arguments:
- patches: bfloat16 [72, 4, 4096], P('var', None, 'tok'), may hold values from -6 to 6
- slot_var: int32 [72], replicated, may hold values from -1 to 47, as said below
- patch_weight: bfloat16 [48, 4, 1024], replicated, may hold values from -3 to 3
- var_embed: bfloat16 [48, 1024], replicated, may hold values from -6 to 6
- query: bfloat16 [1024], replicated, may hold values from -16 to 16
- key_weight: bfloat16 [1024, 1024], P('tok'), may hold values from -0.1875 to 0.1875
- value_weight: bfloat16 [1024, 1024], P('tok'), may hold values from -0.1875 to 0.1875
- out_weight: bfloat16 [1024, 1024], P('tok'), may hold values from -0.1875 to 0.1875
- cotangent: bfloat16 [4096, 1024], P(('tok', 'var')), may hold values from -6 to 6
Outputs:
- aggregated: bfloat16 [4096, 1024], P(('tok', 'var'))
- patch_grad: float32 [72, 4096], P('var', 'tok')
Inputs may be any that keep to these rules, and one draw needn't show every extreme that they name: `slot_var`: slot 9 * i + j belongs to index i of var. Every variable id stands in exactly one slot; empty slots hold -1. The live slots of an index come first and hold consecutive ids, rising from index to index. Every index holds at least one and at most 9 live slots, and some index holds exactly 9.
All inputs are finite; a program needn't handle non-finite values.
Results may differ from a plain program's by a relative error of at most 0.011.
Values may be sent and summed in bfloat16 or wider, within the bound.
No kernel may reach another device: no remote copies, remote signals or barrier semaphores. Data moves between devices by JAX's collectives and lax.ppermute only.
A program may use at most 128 MiB of HBM per device.

v0:
```python
import math
import jax
import jax.numpy as jnp
from jax import lax
from jax.sharding import PartitionSpec as P

H = 16
HD = 64
score_cap = 5.0
inv_sqrt_two = 1.0 / math.sqrt(2.0)
inv_sqrt_two_pi = 1.0 / math.sqrt(2.0 * math.pi)
f32 = jnp.float32
bf16 = jnp.bfloat16


def gelu_exact(inputs):
    return 0.5 * inputs * (1.0 + lax.erf(inputs * inv_sqrt_two))


def gelu_slope(inputs):
    return (
        0.5 * (1.0 + lax.erf(inputs * inv_sqrt_two))
        + inputs * jnp.exp(-0.5 * inputs * inputs) * inv_sqrt_two_pi
    )


def live_index(slot_var, var_total):
    ids = jnp.arange(var_total, dtype=jnp.int32)
    places = jnp.arange(slot_var.shape[0], dtype=jnp.int32)
    match = slot_var[None, :] == ids[:, None]
    return jnp.sum(jnp.where(match, places[None, :], 0), axis=1)


def split(x):
    hi = x.astype(bf16)
    lo = (x - hi.astype(f32)).astype(bf16)
    return (hi, lo)


def ein(spec, a, b):
    return jnp.einsum(spec, a, b, preferred_element_type=f32)


def body(
    patches,
    slot_var,
    patch_weight,
    var_embed,
    query,
    key_weight,
    value_weight,
    out_weight,
    cotangent,
    *,
    n_var,
    n_tok
):
    var_total, pixels_per, width = patch_weight.shape
    local_slots = patches.shape[0]
    rows = key_weight.shape[0]
    tok_count = cotangent.shape[0]
    query_heads = query.reshape(H, HD).astype(f32)
    wq_rows = jnp.sum(key_weight.reshape(rows, H, HD).astype(f32) * query_heads[None], axis=2)
    wq_copies = jnp.broadcast_to(wq_rows[None], (n_tok, rows, H))
    wq_full = lax.all_to_all(wq_copies, "tok", 0, 0, tiled=True).reshape(n_tok * rows, H)
    wq_hi, wq_lo = split(wq_full)
    full = lax.all_gather(jnp.stack([value_weight, out_weight]), "tok", axis=1, tiled=True)
    value_matrix = full[0]
    out_matrix = full[1]
    slot_pixels = lax.all_to_all(patches, "var", 2, 0, tiled=True)
    live_slot = live_index(slot_var, var_total)
    pixels = jnp.take(slot_pixels, live_slot, axis=0)
    pre_act = ein("vpt,vpd->vtd", pixels, patch_weight) + var_embed.astype(f32)[:, None, :]
    embedded = gelu_exact(pre_act).astype(bf16)
    raw_scores = (
        ein("vtd,dh->tvh", embedded, wq_hi) + ein("vtd,dh->tvh", embedded, wq_lo)
    ) / math.sqrt(HD)
    squashed = jnp.tanh(raw_scores / score_cap)
    exp_scores = jnp.exp(score_cap * squashed)
    attn_f32 = exp_scores / jnp.sum(exp_scores, axis=1, keepdims=True)
    attn_bf = attn_f32.astype(bf16)
    value_heads = value_matrix.reshape(width, H, HD)
    mixed_in = ein("tvh,vtd->thd", attn_bf, embedded)
    mix_hi, mix_lo = split(mixed_in)
    pooled = (
        (ein("thd,dhj->thj", mix_hi, value_heads) + ein("thd,dhj->thj", mix_lo, value_heads))
        .astype(bf16)
        .reshape(tok_count, width)
    )
    mixed_out = jnp.dot(pooled, out_matrix, preferred_element_type=f32).astype(bf16)
    contract = (((1,), (1,)), ((), ()))
    grad_pooled = (
        lax.dot_general(cotangent, out_matrix, contract, preferred_element_type=f32)
        .astype(bf16)
        .reshape(tok_count, H, HD)
    )
    spread = ein("thj,dhj->thd", grad_pooled, value_heads)
    spread_hi, spread_lo = split(spread)
    grad_attn = ein("vtd,thd->tvh", embedded, spread_hi) + ein("vtd,thd->tvh", embedded, spread_lo)
    grad_scores = attn_f32 * (grad_attn - jnp.sum(attn_f32 * grad_attn, axis=1, keepdims=True))
    grad_raw = grad_scores * (1.0 - squashed * squashed) / math.sqrt(HD)
    raw_hi, raw_lo = split(grad_raw)
    grad_embed = (
        ein("tvh,thd->vtd", attn_bf, spread_hi)
        + ein("tvh,thd->vtd", attn_bf, spread_lo)
        + ein("tvh,dh->vtd", raw_hi, wq_hi)
        + ein("tvh,dh->vtd", raw_hi, wq_lo)
        + ein("tvh,dh->vtd", raw_lo, wq_hi)
    ).astype(bf16)
    grad_pre = grad_embed.astype(f32) * gelu_slope(pre_act)
    partial = jnp.einsum(
        "vpt,vtd->vpd", pixels.astype(f32), grad_pre, precision=lax.Precision.HIGHEST
    ).reshape(var_total, pixels_per * width)
    slots = n_var * local_slots
    cols = partial.shape[1] // n_tok
    safe = jnp.clip(slot_var, 0, var_total - 1)
    slot_rows = jnp.where((slot_var >= 0)[:, None], jnp.take(partial, safe, axis=0), 0.0)
    blocks = slot_rows.reshape(n_var, local_slots, n_tok, cols).transpose(0, 2, 1, 3)
    by_var = lax.all_to_all(blocks, "var", 0, 0, tiled=True).sum(axis=0)
    by_tok = lax.all_to_all(by_var, "tok", 0, 0, tiled=True).sum(axis=0)
    del slots
    return (mixed_out, by_tok)


def solution(mesh):
    import functools

    fn = functools.partial(body, n_var=mesh.shape["var"], n_tok=mesh.shape["tok"])
    return jax.shard_map(
        fn,
        mesh=mesh,
        in_specs=(
            P("var", None, "tok"),
            P(),
            P(),
            P(),
            P(),
            P("tok", None),
            P("tok", None),
            P("tok", None),
            P(("tok", "var"), None),
        ),
        out_specs=(P(("tok", "var"), None), P("var", "tok")),
        check_vma=False,
    )
```

profile of v0, /device:TPU:32, one launch (start us, length us, event | category | flops | bytes accessed | tf_op | source)
XLA Modules:
  0.0 189.6 jit_solution(7815867198240021874)
XLA Ops:
  10.5 4.5 %all-to-all-start.1 = ((bf16[8,2,288]{2,1,0:T(2,128)(2,1)}), bf16[8,2,288]{2,1,0:T(2,128)(2,1)S(1)}, u32[]{:S(2)}, u32[]{:S(2)}) async-start(bf16[8,2,288]{2,1,0:T(2,128)(2,1)} %reshape.93), calls=%async_computation.1 | async-start | bytes 24576 | tf_op jit(solution)/shard_map/all_to_all | solution.py:70
  20.9 11.2 %all-to-all-start = ((f32[32,1,512]{2,1,0:T(1,128)}), f32[32,1,512]{2,1,0:T(1,128)S(1)}, u32[]{:S(2)}, u32[]{:S(2)}) async-start(f32[32,1,512]{2,1,0:T(1,128)} %reshape.95), calls=%async_computation | async-start | bytes 131072 | tf_op jit(solution)/shard_map/all_to_all | solution.py:65
  33.4 2.9 %multiply_convert_fusion = (bf16[48,16,1024]{2,1,0:T(8,128)(2,1)S(1)}, f32[48,16,1024]{2,1,0:T(8,128)}) fusion(f32[48,1024]{1,0:T(8,128)S(1)} %convert_element_type.88, bf16[48,4,1024]{2,1,0:T(4,128)(2,1)S(1)} %copy-done, bf16[48,4,16]{2,1,0:T(4,128)(2,1)S(1)} %gather_fusion, pred[48]{0:T(512)(128)(4,1)S(1)} %compare_and_fusion.1), kind=kOutput, calls=%fused_computation.17 | convolution fusion | flops 11013120 | bytes 5314608 | tf_op jit(solution)/shard_map/vpt,vpd->vtd/dot_general | solution.py:41
  36.4 5.1 %all-to-all-done = f32[32,1,512]{2,1,0:T(1,128)S(1)} async-done(((f32[32,1,512]{2,1,0:T(1,128)}), f32[32,1,512]{2,1,0:T(1,128)S(1)}, u32[]{:S(2)}, u32[]{:S(2)}) %all-to-all-start) | async-done | bytes 65568 | tf_op jit(solution)/shard_map/all_to_all | solution.py:65
  46.6 48.1 %all-gather.2.cloned.1.call-done = bf16[2,1024,1024]{2,1,0:T(8,128)(2,1)} async-done(((bf16[2,32,1024]{2,1,0:T(8,128)(2,1)}), bf16[2,1024,1024]{2,1,0:T(8,128)(2,1)}) %all-gather.2.cloned.1.call-update) | async-done | bytes 4194320 | tf_op jit(solution)/shard_map/all_gather | solution.py:67
  94.7 3.1 %slice.12 = bf16[1,1024,1024]{2,1,0:T(8,128)(2,1)} slice(bf16[2,1024,1024]{2,1,0:T(8,128)(2,1)} %all-gather.2.cloned.1.call-done), slice={[0:1], [0:1024], [0:1024]} | slice | bytes 4194304 | tf_op jit(solution)/shard_map/slice | solution.py:68
  97.8 3.0 %copy.107 = bf16[1,1024,1024]{1,2,0:T(8,128)(2,1)S(1)} copy(bf16[1,1024,1024]{2,1,0:T(8,128)(2,1)} %slice.12) | data formatting | bytes 4194304 | tf_op jit(solution)/shard_map/slice | solution.py:68
  100.9 2.2 %fusion.28 = bf16[16,1024]{1,0:T(8,128)(2,1)S(1)} fusion(bf16[16,1024]{1,0:T(8,128)(2,1)S(1)} %copy-done.20, bf16[2,1024,1024]{2,1,0:T(8,128)(2,1)} %all-gather.2.cloned.1.call-done), kind=kOutput, calls=%fused_computation.42 | convolution fusion | flops 33570816 | bytes 2162688 | tf_op jit(solution)/shard_map/dot_general | solution.py:93
  106.8 2.6 %convolution_add_fusion.2 = f32[16,48,16]{1,2,0:T(8,128)S(1)} fusion(f32[16,48,16]{1,2,0:T(8,128)S(1)} %fusion.30, bf16[48,16,1024]{2,1,0:T(8,128)(2,1)S(1)} %copy-done.2, bf16[16,16,1024]{2,0,1:T(8,128)(2,1)S(1)} %get-tuple-element.8), kind=kOutput, calls=%fused_computation.37 | convolution fusion | flops 25178112 | bytes 2195456 | tf_op jit(solution)/shard_map/vtd,thd->tvh/dot_general | solution.py:41
  109.4 1.9 %subtract_convert_fusion.2 = (bf16[16,48,16]{1,2,0:T(8,128)(2,1)}, bf16[16,48,16]{1,2,0:T(8,128)(2,1)}) fusion(f32[16,48,16]{1,0,2:T(8,128)S(1)} %copy-done.15, f32[16,48,16]{1,2,0:T(8,128)S(1)} %convolution_add_fusion.2, f32[16,16]{1,0:T(8,128)S(1)} %get-tuple-element.13), kind=kOutput, calls=%fused_computation.67 | output fusion | flops 184623 | bytes 148480 | tf_op jit(solution)/shard_map/sub | solution.py:100
  111.3 1.7 copy.128
  113.0 3.3 %fusion.56 = f32[1024,16,48]{0,1,2:T(8,128)} fusion(bf16[16,48,16]{2,0,1:T(8,128)(2,1)} %copy.128, f32[1024,16]{0,1:T(8,128)} %copy-done.5), kind=kOutput, calls=%fused_computation.84 | convolution fusion | flops 25231360 | bytes 3235840 | tf_op jit(solution)/shard_map/tvh,dh->vtd/dot_general | solution.py:41
  116.4 2.3 %fusion.50 = f32[1024,16,48]{0,1,2:T(8,128)} fusion(bf16[16,48,16]{2,0,1:T(8,128)(2,1)S(1)} %copy-done.4, f32[1024,16]{0,1:T(8,128)S(1)} %copy-done.6), kind=kOutput, calls=%fused_computation.76 | convolution fusion | flops 25182208 | bytes 3235840 | tf_op jit(solution)/shard_map/tvh,dh->vtd/dot_general | solution.py:41
  118.7 2.2 %fusion.41 = f32[16,1024,48]{1,2,0:T(8,128)} fusion(bf16[16,48,16]{1,2,0:T(8,128)(2,1)S(1)} %copy-done.8, bf16[16,16,1024]{2,0,1:T(8,128)(2,1)S(1)} %get-tuple-element.8), kind=kOutput, calls=%fused_computation.57 | convolution fusion | flops 25165824 | bytes 3694592 | tf_op jit(solution)/shard_map/tvh,thd->vtd/dot_general | solution.py:41
  120.9 2.3 %fusion.44 = f32[16,1024,48]{1,2,0:T(8,128)} fusion(bf16[16,48,16]{1,2,0:T(8,128)(2,1)S(1)} %copy-done.8, bf16[16,16,1024]{2,0,1:T(8,128)(2,1)S(1)} %get-tuple-element.9), kind=kOutput, calls=%fused_computation.60 | convolution fusion | flops 25165824 | bytes 3694592 | tf_op jit(solution)/shard_map/tvh,thd->vtd/dot_general | solution.py:41
  123.4 8.5 %fusion.8 = bf16[48,16,1024]{2,1,0:T(8,128)(2,1)S(1)} fusion(f32[1024,16,48]{0,1,2:T(8,128)} %fusion.56, f32[1024,16,48]{0,1,2:T(8,128)} %fusion.50, f32[16,1024,48]{1,2,0:T(8,128)} %fusion.41, f32[16,1024,48]{1,2,0:T(8,128)} %fusion.44, bf16[16,48,16]{2,0,1:T(8,128)(2,1)S(1)} %copy.130, f32[1024,16]{0,1:T(8,128)S(1)} %copy-done.7), kind=kOutput, calls=%fused_computation.11 | convolution fusion | flops 29114368 | bytes 14245888 | tf_op jit(solution)/shard_map/tvh,dh->vtd/dot_general | solution.py:41
  131.9 3.2 %fusion.6 = f32[48,4,1024]{2,1,0:T(4,128)S(1)} fusion(bf16[48,16,1024]{2,1,0:T(8,128)(2,1)S(1)} %fusion.8, f32[48,16,1024]{2,1,0:T(8,128)S(1)} %copy-done.3, f32[48,1024]{1,0:T(8,128)S(1)} %copy-done.11, bf16[48,4,16]{2,1,0:T(4,128)(2,1)S(1)} %copy-done.13, pred[48]{0:T(512)(128)(4,1)S(1)} %copy-done.19), kind=kOutput, calls=%fused_computation.9 | convolution fusion | flops 46402560 | bytes 5707824 | tf_op jit(solution)/shard_map/vpt,vtd->vpd/dot_general | solution.py:111
  135.6 2.0 %gather_fusion.1 = f32[72,4096]{1,0:T(8,128)} fusion(f32[48,4096]{1,0:T(8,128)S(1)} %bitcast.98, s32[1024]{0:T(1024)S(1)} %pad_clamp_fusion), kind=kCustom, calls=%fused_computation.1 | custom fusion | bytes 2359584 | tf_op jit(solution)/shard_map/jit(_take)/gather | solution.py:117
  140.4 4.3 %all-to-all-start.2 = ((f32[8,32,9,128]{3,1,2,0:T(8,128)}), f32[8,32,9,128]{3,1,2,0:T(8,128)}, u32[]{:S(2)}, u32[]{:S(2)}) async-start(f32[8,32,9,128]{3,1,2,0:T(8,128)} %select_bitcast_fusion), calls=%async_computation.2 | async-start | bytes 2359296 | tf_op jit(solution)/shard_map/all_to_all | solution.py:119
  144.7 3.2 %subtract_convert_fusion.1 = (bf16[16,16,1024]{2,1,0:T(8,128)(2,1)S(1)}, bf16[16,16,1024]{2,1,0:T(8,128)(2,1)S(1)}) fusion(bf16[16,48,16]{1,2,0:T(8,128)(2,1)S(1)} %copy-done.9, bf16[48,16,1024]{2,1,0:T(8,128)(2,1)} %copy-done.1), kind=kOutput, calls=%fused_computation.44 | convolution fusion | flops 26214400 | bytes 2646016 | tf_op jit(solution)/shard_map/tvh,vtd->thd/dot_general | solution.py:41
  148.5 13.6 %all-to-all-done.2 = f32[8,32,9,128]{3,1,2,0:T(8,128)} async-done(((f32[8,32,9,128]{3,1,2,0:T(8,128)}), f32[8,32,9,128]{3,1,2,0:T(8,128)}, u32[]{:S(2)}, u32[]{:S(2)}) %all-to-all-start.2) | async-done | bytes 1179680 | tf_op jit(solution)/shard_map/all_to_all | solution.py:119
  164.3 5.8 %all-to-all-start.3 = ((f32[32,9,128]{2,1,0:T(8,128)}), f32[32,9,128]{2,1,0:T(8,128)S(1)}, u32[]{:S(2)}, u32[]{:S(2)}) async-start(f32[32,9,128]{2,1,0:T(8,128)} %copy.131), calls=%async_computation.3 | async-start | bytes 524288 | tf_op jit(solution)/shard_map/all_to_all | solution.py:120
  170.9 2.6 %fusion.26 = bf16[16,1024]{1,0:T(8,128)(2,1)} fusion(bf16[16,1024]{1,0:T(8,128)(2,1)S(1)} %reshape.69, bf16[2,1024,1024]{2,1,0:T(8,128)(2,1)} %all-gather.2.cloned.1.call-done), kind=kOutput, calls=%fused_computation.40 | convolution fusion | flops 33570816 | bytes 2162688 | tf_op jit(solution)/shard_map/dot_general | solution.py:90
  173.5 8.6 %all-to-all-done.3 = f32[32,9,128]{2,1,0:T(8,128)S(1)} async-done(((f32[32,9,128]{2,1,0:T(8,128)}), f32[32,9,128]{2,1,0:T(8,128)S(1)}, u32[]{:S(2)}, u32[]{:S(2)}) %all-to-all-start.3) | async-done | bytes 147488 | tf_op jit(solution)/shard_map/all_to_all | solution.py:120
  (89 shorter events, 27.0 us)
Async XLA Ops:
  7.2 26.2 %copy-start = (bf16[48,4,1024]{2,1,0:T(4,128)(2,1)S(1)}, bf16[48,4,1024]{2,1,0:T(4,128)(2,1)}, u32[]{:S(2)}) copy-start(bf16[48,4,1024]{2,1,0:T(4,128)(2,1)} %param.11) | copy-start | bytes 1179652
  7.2 87.5 %all-gather.2.cloned.1.call-start = ((), (), s32[]{:S(2)}) async-start(), calls=%async_computation.4 | async-start | bytes 4325376 | tf_op jit(solution)/shard_map/all_gather | solution.py:67
  10.5 10.4 %all-to-all-start.1 = ((bf16[8,2,288]{2,1,0:T(2,128)(2,1)}), bf16[8,2,288]{2,1,0:T(2,128)(2,1)S(1)}, u32[]{:S(2)}, u32[]{:S(2)}) async-start(bf16[8,2,288]{2,1,0:T(2,128)(2,1)} %reshape.93), calls=%async_computation.1 | async-start | bytes 24576 | tf_op jit(solution)/shard_map/all_to_all | solution.py:70
  17.7 18.6 %copy-start.18 = (pred[48]{0:T(512)(128)(4,1)}, pred[48]{0:T(512)(128)(4,1)S(1)}, u32[]{:S(2)}) copy-start(pred[48]{0:T(512)(128)(4,1)S(1)} %compare_and_fusion.1) | copy-start | bytes 148
  19.3 17.0 %copy-start.10 = (f32[48,1024]{1,0:T(8,128)}, f32[48,1024]{1,0:T(8,128)S(1)}, u32[]{:S(2)}) copy-start(f32[48,1024]{1,0:T(8,128)S(1)} %convert_element_type.88) | copy-start | bytes 589828
  20.9 20.6 %all-to-all-start = ((f32[32,1,512]{2,1,0:T(1,128)}), f32[32,1,512]{2,1,0:T(1,128)S(1)}, u32[]{:S(2)}, u32[]{:S(2)}) async-start(f32[32,1,512]{2,1,0:T(1,128)} %reshape.95), calls=%async_computation | async-start | bytes 131072 | tf_op jit(solution)/shard_map/all_to_all | solution.py:65
  33.4 8.0 %copy-start.12 = (bf16[48,4,16]{2,1,0:T(4,128)(2,1)}, bf16[48,4,16]{2,1,0:T(4,128)(2,1)S(1)}, u32[]{:S(2)}) copy-start(bf16[48,4,16]{2,1,0:T(4,128)(2,1)S(1)} %gather_fusion) | copy-start | bytes 18436
  36.4 58.3 %copy-start.1 = (bf16[48,16,1024]{2,1,0:T(8,128)(2,1)}, bf16[48,16,1024]{2,1,0:T(8,128)(2,1)S(1)}, u32[]{:S(2)}) copy-start(bf16[48,16,1024]{2,1,0:T(8,128)(2,1)S(1)} %get-tuple-element.11) | copy-start | bytes 4718596
  43.1 51.6 %copy-start.5 = (f32[1024,16]{0,1:T(8,128)}, f32[1024,16]{0,1:T(8,128)S(1)}, u32[]{:S(2)}) copy-start(f32[1024,16]{0,1:T(8,128)S(1)} %reshape.68) | copy-start | bytes 196612
  46.6 54.3 %copy-start.20 = (bf16[16,1024]{1,0:T(8,128)(2,1)S(1)}, bf16[16,1024]{1,0:T(8,128)(2,1)}, u32[]{:S(2)}) copy-start(bf16[16,1024]{1,0:T(8,128)(2,1)} %param.17) | copy-start | bytes 98308
  105.2 4.2 %copy-start.15 = (f32[16,48,16]{1,0,2:T(8,128)S(1)}, f32[16,48,16]{1,0,2:T(8,128)}, u32[]{:S(2)}) copy-start(f32[16,48,16]{1,0,2:T(8,128)} %copy-done.14) | copy-start | bytes 147460
  113.0 3.3 %copy-start.4 = (bf16[16,48,16]{2,0,1:T(8,128)(2,1)S(1)}, bf16[16,48,16]{2,0,1:T(8,128)(2,1)}, u32[]{:S(2)}) copy-start(bf16[16,48,16]{2,0,1:T(8,128)(2,1)} %copy.128) | copy-start | bytes 73732
  113.0 3.3 %copy-start.6 = (f32[1024,16]{0,1:T(8,128)S(1)}, f32[1024,16]{0,1:T(8,128)}, u32[]{:S(2)}) copy-start(f32[1024,16]{0,1:T(8,128)} %copy-done.5) | copy-start | bytes 196612
  113.0 5.6 %copy-start.8 = (bf16[16,48,16]{1,2,0:T(8,128)(2,1)S(1)}, bf16[16,48,16]{1,2,0:T(8,128)(2,1)}, u32[]{:S(2)}) copy-start(bf16[16,48,16]{1,2,0:T(8,128)(2,1)} %fusion.59) | copy-start | bytes 73732
  120.9 2.3 %copy-start.16 = (bf16[16,48,16]{1,2,0:T(8,128)(2,1)S(1)}, bf16[16,48,16]{1,2,0:T(8,128)(2,1)}, u32[]{:S(2)}) copy-start(bf16[16,48,16]{1,2,0:T(8,128)(2,1)} %get-tuple-element.4) | copy-start | bytes 73732
  120.9 2.5 %copy-start.7 = (f32[1024,16]{0,1:T(8,128)S(1)}, f32[1024,16]{0,1:T(8,128)}, u32[]{:S(2)}) copy-start(f32[1024,16]{0,1:T(8,128)} %copy-done.5) | copy-start | bytes 196612
  123.4 8.5 %copy-start.3 = (f32[48,16,1024]{2,1,0:T(8,128)S(1)}, f32[48,16,1024]{2,1,0:T(8,128)}, u32[]{:S(2)}) copy-start(f32[48,16,1024]{2,1,0:T(8,128)} %get-tuple-element.12) | copy-start | bytes 9437188
  123.4 8.5 %copy-start.11 = (f32[48,1024]{1,0:T(8,128)S(1)}, f32[48,1024]{1,0:T(8,128)}, u32[]{:S(2)}) copy-start(f32[48,1024]{1,0:T(8,128)} %copy-done.10) | copy-start | bytes 589828
  123.4 8.5 %copy-start.13 = (bf16[48,4,16]{2,1,0:T(4,128)(2,1)S(1)}, bf16[48,4,16]{2,1,0:T(4,128)(2,1)}, u32[]{:S(2)}) copy-start(bf16[48,4,16]{2,1,0:T(4,128)(2,1)} %copy-done.12) | copy-start | bytes 18436
  123.4 8.5 %copy-start.19 = (pred[48]{0:T(512)(128)(4,1)S(1)}, pred[48]{0:T(512)(128)(4,1)}, u32[]{:S(2)}) copy-start(pred[48]{0:T(512)(128)(4,1)} %copy-done.18) | copy-start | bytes 148
  135.6 3.5 %copy-start.17 = (pred[8,9]{1,0:T(8,128)(4,1)S(1)}, pred[8,9]{1,0:T(8,128)(4,1)}, u32[]{:S(2)}) copy-start(pred[8,9]{1,0:T(8,128)(4,1)} %broadcast_in_dim.69) | copy-start | bytes 220
  137.6 7.1 %copy-start.9 = (bf16[16,48,16]{1,2,0:T(8,128)(2,1)S(1)}, bf16[16,48,16]{1,2,0:T(8,128)(2,1)}, u32[]{:S(2)}) copy-start(bf16[16,48,16]{1,2,0:T(8,128)(2,1)} %fusion.59) | copy-start | bytes 73732
  140.4 21.7 %all-to-all-start.2 = ((f32[8,32,9,128]{3,1,2,0:T(8,128)}), f32[8,32,9,128]{3,1,2,0:T(8,128)}, u32[]{:S(2)}, u32[]{:S(2)}) async-start(f32[8,32,9,128]{3,1,2,0:T(8,128)} %select_bitcast_fusion), calls=%async_computation.2 | async-start | bytes 2359296 | tf_op jit(solution)/shard_map/all_to_all | solution.py:119
  164.3 17.8 %all-to-all-start.3 = ((f32[32,9,128]{2,1,0:T(8,128)}), f32[32,9,128]{2,1,0:T(8,128)S(1)}, u32[]{:S(2)}, u32[]{:S(2)}) async-start(f32[32,9,128]{2,1,0:T(8,128)} %copy.131), calls=%async_computation.3 | async-start | bytes 524288 | tf_op jit(solution)/shard_map/all_to_all | solution.py:120
  (2 other events, 2.1 us)
Sparse Core Ops, SparseCore 0:
  10.6 84.0 all-gather.1
where the time goes:
time: 190 us
  waiting for transfers between devices  75.3 us (40%)
  matrix products  41.6 us (22%)
  starting transfers between devices  25.8 us (14%)
  local copies, waits for them, and re-layouts  21.7 us (11%)
  between operations  14.4 us (8%)
  other arithmetic  10.8 us (6%)
    all_gather x1, waiting for transfers between devices, body(): lax.all_gather(jnp.stack([value_weight, out_weight]), 'tok', axis=1, tile...  48.1 us
    dot_general x14, matrix products, ein(): return jnp.einsum(spec, a, b, preferred_element_type=f32)  33.6 us
    all_to_all x1, waiting for transfers between devices, body(): by_var = lax.all_to_all(blocks, 'var', 0, 0, tiled=True).sum(axis=0)  13.6 us
    all_to_all x1, starting transfers between devices, body(): lax.all_to_all(wq_copies, 'tok', 0, 0, tiled=True).reshape(n_tok * rows, H)  11.2 us
    all_to_all x1, waiting for transfers between devices, body(): by_tok = lax.all_to_all(by_var, 'tok', 0, 0, tiled=True).sum(axis=0)  8.57 us
    slice x2, local copies, waits for them, and re-layouts, body(): value_matrix = full[0]  6.18 us
    all_to_all x1, starting transfers between devices, body(): by_tok = lax.all_to_all(by_var, 'tok', 0, 0, tiled=True).sum(axis=0)  5.8 us
    unnamed x50, local copies, waits for them, and re-layouts  5.65 us
  transfers between devices with their start and end apart: 5, of which 4 were waited for; matrix products, arithmetic and copies ran while one was open for 12% of the time, Pallas kernels for 0%

commit v1 on v0

--- a/solution.py
+++ b/solution.py
@@ -64,7 +64,12 @@
     wq_copies = jnp.broadcast_to(wq_rows[None], (n_tok, rows, H))
     wq_full = lax.all_to_all(wq_copies, "tok", 0, 0, tiled=True).reshape(n_tok * rows, H)
     wq_hi, wq_lo = split(wq_full)
-    full = lax.all_gather(jnp.stack([value_weight, out_weight]), "tok", axis=1, tiled=True)
+    full = jnp.concatenate(
+        lax.all_to_all(
+            jnp.stack([jnp.stack([value_weight, out_weight])] * lax.axis_size("tok")), "tok", 0, 0
+        ),
+        axis=1,
+    )
     value_matrix = full[0]
     out_matrix = full[1]
     slot_pixels = lax.all_to_all(patches, "var", 2, 0, tiled=True)

time: 190 us -> 231 us (1.22)
  waiting for transfers between devices: 75.3 us -> 117 us
  between operations: 14.4 us -> 1.05 us
  local copies, waits for them, and re-layouts: 21.7 us -> 31.1 us
  starting transfers between devices: 25.8 us -> 31.8 us
  other arithmetic: 10.8 us -> 7.87 us
    all_to_all x0 -> x1, waiting for transfers between devices: none -> 83.9 us  [body(): lax.all_to_all(jnp.stack([jnp.stack([value_weight, out_weight])] * lax.ax...]
    all_gather x1 -> x0, waiting for transfers between devices: 48.1 us -> none  [body(): lax.all_gather(jnp.stack([value_weight, out_weight]), 'tok', axis=1, tile...]
    another operation x0 -> x3, local copies, waits for them, and re-layouts: none -> 11.1 us  [the longest x2 8.61 us: body(): value_heads = value_matrix.reshape(width, H, HD)]
    all_to_all x0 -> x1, starting transfers between devices: none -> 5.73 us  [body(): lax.all_to_all(jnp.stack([jnp.stack([value_weight, out_weight])] * lax.ax...]
    slice x2 -> x1, local copies, waits for them, and re-layouts: 6.18 us -> 1.8 us  [body(): out_matrix = full[1]]
    all_to_all x1, waiting for transfers between devices: 5.08 us -> 8.21 us  [body(): lax.all_to_all(wq_copies, 'tok', 0, 0, tiled=True).reshape(n_tok * rows, H)]
    all_to_all x0 -> x1, local copies, waits for them, and re-layouts: none -> 2.63 us  [body(): lax.all_to_all(jnp.stack([jnp.stack([value_weight, out_weight])] * lax.ax...]
    all_to_all x1, waiting for transfers between devices: 0.01 us -> 2.57 us  [body(): slot_pixels = lax.all_to_all(patches, 'var', 2, 0, tiled=True)]
  transfers between devices with their start and end apart: 5 -> 5, of which waited for: 4 -> 5; matrix products, arithmetic and copies ran while one was open for 12% -> 9% of each run, Pallas kernels for 0% -> 0%
where the time goes in v1:
time: 231 us; the launch traced here: 230 us
  waiting for transfers between devices  117 us (51%)
  matrix products  41.5 us (18%)
  starting transfers between devices  31.8 us (14%)
  local copies, waits for them, and re-layouts  31.1 us (13%)
  other arithmetic  7.87 us (3%)
    all_to_all x1, waiting for transfers between devices, body(): lax.all_to_all(jnp.stack([jnp.stack([value_weight, out_weight])] * lax.ax...  83.9 us
    dot_general x14, matrix products, ein(): return jnp.einsum(spec, a, b, preferred_element_type=f32)  33.5 us
    all_to_all x1, waiting for transfers between devices, body(): by_var = lax.all_to_all(blocks, 'var', 0, 0, tiled=True).sum(axis=0)  13.5 us
    all_to_all x1, starting transfers between devices, body(): lax.all_to_all(wq_copies, 'tok', 0, 0, tiled=True).reshape(n_tok * rows, H)  11.2 us
    another operation x2, local copies, waits for them, and re-layouts, body(): value_heads = value_matrix.reshape(width, H, HD)  8.61 us
    all_to_all x1, waiting for transfers between devices, body(): by_tok = lax.all_to_all(by_var, 'tok', 0, 0, tiled=True).sum(axis=0)  8.58 us
    all_to_all x1, waiting for transfers between devices, body(): lax.all_to_all(wq_copies, 'tok', 0, 0, tiled=True).reshape(n_tok * rows, H)  8.21 us
    all_to_all x1, starting transfers between devices, body(): by_tok = lax.all_to_all(by_var, 'tok', 0, 0, tiled=True).sum(axis=0)  6.12 us
  transfers between devices with their start and end apart: 5, of which 5 were waited for; matrix products, arithmetic and copies ran while one was open for 9% of the time, Pallas kernels for 0%

profile of v1, /device:TPU:32, one launch (start us, length us, event | category | flops | bytes accessed | tf_op | source)
XLA Modules:
  0.0 230.1 jit_solution(16088340792761794618)
XLA Ops:
  2.4 4.5 %all-to-all-start.2 = ((bf16[8,2,288]{2,1,0:T(2,128)(2,1)}), bf16[8,2,288]{2,1,0:T(2,128)(2,1)S(1)}, u32[]{:S(2)}, u32[]{:S(2)}) async-start(bf16[8,2,288]{2,1,0:T(2,128)(2,1)} %reshape.104), calls=%async_computation.2 | async-start | bytes 24576 | tf_op jit(solution)/shard_map/all_to_all | solution.py:75
  9.6 2.6 %all-to-all-done.2 = bf16[8,2,288]{2,1,0:T(2,128)(2,1)S(1)} async-done(((bf16[8,2,288]{2,1,0:T(2,128)(2,1)}), bf16[8,2,288]{2,1,0:T(2,128)(2,1)S(1)}, u32[]{:S(2)}, u32[]{:S(2)}) %all-to-all-start.2) | async-done | bytes 9248 | tf_op jit(solution)/shard_map/all_to_all | solution.py:75
  12.2 11.2 %all-to-all-start.1 = ((f32[32,1,512]{2,1,0:T(1,128)}), f32[32,1,512]{2,1,0:T(1,128)S(1)}, u32[]{:S(2)}, u32[]{:S(2)}) async-start(f32[32,1,512]{2,1,0:T(1,128)} %reshape.106), calls=%async_computation.1 | async-start | bytes 131072 | tf_op jit(solution)/shard_map/all_to_all | solution.py:65
  24.2 8.2 %all-to-all-done.1 = f32[32,1,512]{2,1,0:T(1,128)S(1)} async-done(((f32[32,1,512]{2,1,0:T(1,128)}), f32[32,1,512]{2,1,0:T(1,128)S(1)}, u32[]{:S(2)}, u32[]{:S(2)}) %all-to-all-start.1) | async-done | bytes 65568 | tf_op jit(solution)/shard_map/all_to_all | solution.py:65
  32.5 2.5 %stack.11 = bf16[32,2,32,1024]{3,2,1,0:T(8,128)(2,1)} broadcast(bf16[2,32,1024]{2,1,0:T(8,128)(2,1)S(1)} %pad_maximum_fusion), dimensions={1,2,3} | broadcast | bytes 4325376 | tf_op jit(solution)/shard_map/stack | solution.py:69
  35.0 5.7 %all-to-all-start = ((bf16[32,2,32,1024]{3,2,1,0:T(8,128)(2,1)}), bf16[32,2,32,1024]{3,2,1,0:T(8,128)(2,1)}, u32[]{:S(2)}, u32[]{:S(2)}) async-start(bf16[32,2,32,1024]{3,2,1,0:T(8,128)(2,1)} %stack.11), calls=%async_computation | async-start | bytes 8388608 | tf_op jit(solution)/shard_map/all_to_all | solution.py:68
  43.0 2.9 %multiply_convert_fusion = (bf16[48,16,1024]{2,1,0:T(8,128)(2,1)S(1)}, f32[48,16,1024]{2,1,0:T(8,128)}) fusion(f32[48,1024]{1,0:T(8,128)S(1)} %convert_element_type.88, bf16[48,4,1024]{2,1,0:T(4,128)(2,1)S(1)} %copy-done, bf16[48,4,16]{2,1,0:T(4,128)(2,1)S(1)} %gather_fusion, pred[48]{0:T(512)(128)(4,1)S(1)} %compare_and_fusion.1), kind=kOutput, calls=%fused_computation.18 | convolution fusion | flops 11013120 | bytes 5314608 | tf_op jit(solution)/shard_map/vpt,vpd->vtd/dot_general | solution.py:41
  51.2 83.9 %all-to-all-done = bf16[32,2,32,1024]{3,2,1,0:T(8,128)(2,1)} async-done(((bf16[32,2,32,1024]{3,2,1,0:T(8,128)(2,1)}), bf16[32,2,32,1024]{3,2,1,0:T(8,128)(2,1)}, u32[]{:S(2)}, u32[]{:S(2)}) %all-to-all-start) | async-done | bytes 4194336 | tf_op jit(solution)/shard_map/all_to_all | solution.py:68
  135.1 2.6 %copy.184 = bf16[32,2,32,1024]{3,2,0,1:T(8,128)(2,1)S(1)} copy(bf16[32,2,32,1024]{3,2,1,0:T(8,128)(2,1)} %all-to-all-done) | data formatting | bytes 8388608 | tf_op jit(solution)/shard_map/all_to_all | solution.py:68
  139.6 4.0 %reshape_squeeze.3 = bf16[1024,16,64]{2,1,0:T(8,128)(2,1)} reshape(bf16[1,32,32,1024]{3,2,1,0:T(8,128)(2,1)S(1)} %get-tuple-element.9) | data formatting | bytes 4194304 | tf_op jit(solution)/shard_map/reshape;squeeze | solution.py:87
  143.5 4.6 %copy.126 = bf16[1024,16,64]{0,2,1:T(8,128)(2,1)S(1)} copy(bf16[1024,16,64]{2,1,0:T(8,128)(2,1)} %reshape_squeeze.3) | data formatting | bytes 4194304 | tf_op jit(solution)/shard_map/reshape;squeeze | solution.py:87
  154.1 2.6 %convolution_add_fusion.2 = f32[16,48,16]{1,2,0:T(8,128)S(1)} fusion(f32[16,48,16]{1,2,0:T(8,128)S(1)} %fusion.26, bf16[48,16,1024]{2,1,0:T(8,128)(2,1)S(1)} %copy-done.2, bf16[16,16,1024]{2,0,1:T(8,128)(2,1)S(1)} %get-tuple-element.10), kind=kOutput, calls=%fused_computation.35 | convolution fusion | flops 25178112 | bytes 2195456 | tf_op jit(solution)/shard_map/vtd,thd->tvh/dot_general | solution.py:41
  160.3 3.2 %fusion.52 = f32[1024,16,48]{0,1,2:T(8,128)} fusion(bf16[16,48,16]{2,0,1:T(8,128)(2,1)} %copy.141, f32[1024,16]{0,1:T(8,128)} %copy-done.5), kind=kOutput, calls=%fused_computation.82 | convolution fusion | flops 25231360 | bytes 3235840 | tf_op jit(solution)/shard_map/tvh,dh->vtd/dot_general | solution.py:41
  163.6 2.2 fusion.46
  165.8 2.4 %fusion.37 = f32[16,1024,48]{1,2,0:T(8,128)} fusion(bf16[16,48,16]{1,2,0:T(8,128)(2,1)S(1)} %copy-done.8, bf16[16,16,1024]{2,0,1:T(8,128)(2,1)S(1)} %get-tuple-element.10), kind=kOutput, calls=%fused_computation.55 | convolution fusion | flops 25165824 | bytes 3694592 | tf_op jit(solution)/shard_map/tvh,thd->vtd/dot_general | solution.py:41
  168.2 2.3 fusion.40
  170.7 8.5 %fusion.8 = bf16[48,16,1024]{2,1,0:T(8,128)(2,1)S(1)} fusion(f32[1024,16,48]{0,1,2:T(8,128)} %fusion.52, f32[1024,16,48]{0,1,2:T(8,128)} %fusion.46, f32[16,1024,48]{1,2,0:T(8,128)} %fusion.37, f32[16,1024,48]{1,2,0:T(8,128)} %fusion.40, bf16[16,48,16]{2,0,1:T(8,128)(2,1)S(1)} %copy.143, f32[1024,16]{0,1:T(8,128)S(1)} %copy-done.7), kind=kOutput, calls=%fused_computation.12 | convolution fusion | flops 29114368 | bytes 14245888 | tf_op jit(solution)/shard_map/tvh,dh->vtd/dot_general | solution.py:41
  179.2 3.2 %fusion.6 = f32[48,4,1024]{2,1,0:T(4,128)S(1)} fusion(bf16[48,16,1024]{2,1,0:T(8,128)(2,1)S(1)} %fusion.8, f32[48,16,1024]{2,1,0:T(8,128)S(1)} %copy-done.3, f32[48,1024]{1,0:T(8,128)S(1)} %copy-done.11, bf16[48,4,16]{2,1,0:T(4,128)(2,1)S(1)} %copy-done.13, pred[48]{0:T(512)(128)(4,1)S(1)} %copy-done.21), kind=kOutput, calls=%fused_computation.10 | convolution fusion | flops 46402560 | bytes 5707824 | tf_op jit(solution)/shard_map/vpt,vtd->vpd/dot_general | solution.py:116
  187.6 4.3 %all-to-all-start.3 = ((f32[8,32,9,128]{3,1,2,0:T(8,128)}), f32[8,32,9,128]{3,1,2,0:T(8,128)}, u32[]{:S(2)}, u32[]{:S(2)}) async-start(f32[8,32,9,128]{3,1,2,0:T(8,128)} %select_bitcast_fusion), calls=%async_computation.3 | async-start | bytes 2359296 | tf_op jit(solution)/shard_map/all_to_all | solution.py:124
  191.8 3.2 %subtract_convert_fusion.1 = (bf16[16,16,1024]{2,1,0:T(8,128)(2,1)S(1)}, bf16[16,16,1024]{2,1,0:T(8,128)(2,1)S(1)}) fusion(bf16[16,48,16]{1,2,0:T(8,128)(2,1)S(1)} %copy-done.9, bf16[48,16,1024]{2,1,0:T(8,128)(2,1)} %copy-done.1), kind=kOutput, calls=%fused_computation.42 | convolution fusion | flops 26214400 | bytes 2646016 | tf_op jit(solution)/shard_map/tvh,vtd->thd/dot_general | solution.py:41
  195.7 13.5 %all-to-all-done.3 = f32[8,32,9,128]{3,1,2,0:T(8,128)} async-done(((f32[8,32,9,128]{3,1,2,0:T(8,128)}), f32[8,32,9,128]{3,1,2,0:T(8,128)}, u32[]{:S(2)}, u32[]{:S(2)}) %all-to-all-start.3) | async-done | bytes 1179680 | tf_op jit(solution)/shard_map/all_to_all | solution.py:124
  211.3 6.1 %all-to-all-start.4 = ((f32[32,9,128]{2,1,0:T(8,128)}), f32[32,9,128]{2,1,0:T(8,128)S(1)}, u32[]{:S(2)}, u32[]{:S(2)}) async-start(f32[32,9,128]{2,1,0:T(8,128)} %copy.144), calls=%async_computation.4 | async-start | bytes 524288 | tf_op jit(solution)/shard_map/all_to_all | solution.py:125
  218.3 2.6 %convolution_convert_fusion.1 = bf16[16,1024]{1,0:T(8,128)(2,1)} fusion(bf16[16,1024]{1,0:T(8,128)(2,1)S(1)} %reshape.80, bf16[1024,1024]{1,0:T(8,128)(2,1)} %bitcast.97), kind=kOutput, calls=%fused_computation.39 | convolution fusion | flops 33570816 | bytes 2162688 | tf_op jit(solution)/shard_map/dot_general | solution.py:95
  220.9 8.6 %all-to-all-done.4 = f32[32,9,128]{2,1,0:T(8,128)S(1)} async-done(((f32[32,9,128]{2,1,0:T(8,128)}), f32[32,9,128]{2,1,0:T(8,128)S(1)}, u32[]{:S(2)}, u32[]{:S(2)}) %all-to-all-start.4) | async-done | bytes 147488 | tf_op jit(solution)/shard_map/all_to_all | solution.py:125
  (95 shorter events, 33.7 us)
Async XLA Ops:
  0.6 42.4 %copy-start = (bf16[48,4,1024]{2,1,0:T(4,128)(2,1)S(1)}, bf16[48,4,1024]{2,1,0:T(4,128)(2,1)}, u32[]{:S(2)}) copy-start(bf16[48,4,1024]{2,1,0:T(4,128)(2,1)} %param.11) | copy-start | bytes 1179652
  2.4 9.8 %all-to-all-start.2 = ((bf16[8,2,288]{2,1,0:T(2,128)(2,1)}), bf16[8,2,288]{2,1,0:T(2,128)(2,1)S(1)}, u32[]{:S(2)}, u32[]{:S(2)}) async-start(bf16[8,2,288]{2,1,0:T(2,128)(2,1)} %reshape.104), calls=%async_computation.2 | async-start | bytes 24576 | tf_op jit(solution)/shard_map/all_to_all | solution.py:75
  12.2 20.3 %all-to-all-start.1 = ((f32[32,1,512]{2,1,0:T(1,128)}), f32[32,1,512]{2,1,0:T(1,128)S(1)}, u32[]{:S(2)}, u32[]{:S(2)}) async-start(f32[32,1,512]{2,1,0:T(1,128)} %reshape.106), calls=%async_computation.1 | async-start | bytes 131072 | tf_op jit(solution)/shard_map/all_to_all | solution.py:65
  35.0 5.7 %copy-start.16 = (bf16[48,1024]{1,0:T(8,128)(2,1)S(1)}, bf16[48,1024]{1,0:T(8,128)(2,1)}, u32[]{:S(2)}) copy-start(bf16[48,1024]{1,0:T(8,128)(2,1)} %param.12) | copy-start | bytes 294916
  35.0 5.8 %copy-start.22 = (s32[72]{0:T(128)S(1)}, s32[72]{0:T(128)}, u32[]{:S(2)}) copy-start(s32[72]{0:T(128)} %param.10) | copy-start | bytes 868
  35.0 100.1 %all-to-all-start = ((bf16[32,2,32,1024]{3,2,1,0:T(8,128)(2,1)}), bf16[32,2,32,1024]{3,2,1,0:T(8,128)(2,1)}, u32[]{:S(2)}, u32[]{:S(2)}) async-start(bf16[32,2,32,1024]{3,2,1,0:T(8,128)(2,1)} %stack.11), calls=%async_computation | async-start | bytes 8388608 | tf_op jit(solution)/shard_map/all_to_all | solution.py:68
  40.8 5.8 %copy-start.10 = (f32[48,1024]{1,0:T(8,128)}, f32[48,1024]{1,0:T(8,128)S(1)}, u32[]{:S(2)}) copy-start(f32[48,1024]{1,0:T(8,128)S(1)} %convert_element_type.88) | copy-start | bytes 589828
  41.7 4.3 %copy-start.20 = (pred[48]{0:T(512)(128)(4,1)}, pred[48]{0:T(512)(128)(4,1)S(1)}, u32[]{:S(2)}) copy-start(pred[48]{0:T(512)(128)(4,1)S(1)} %compare_and_fusion.1) | copy-start | bytes 148
  43.0 2.9 %copy-start.12 = (bf16[48,4,16]{2,1,0:T(4,128)(2,1)}, bf16[48,4,16]{2,1,0:T(4,128)(2,1)S(1)}, u32[]{:S(2)}) copy-start(bf16[48,4,16]{2,1,0:T(4,128)(2,1)S(1)} %gather_fusion) | copy-start | bytes 18436
  46.0 91.8 %copy-start.1 = (bf16[48,16,1024]{2,1,0:T(8,128)(2,1)}, bf16[48,16,1024]{2,1,0:T(8,128)(2,1)S(1)}, u32[]{:S(2)}) copy-start(bf16[48,16,1024]{2,1,0:T(8,128)(2,1)S(1)} %get-tuple-element.13) | copy-start | bytes 4718596
  47.7 90.1 %copy-start.5 = (f32[1024,16]{0,1:T(8,128)}, f32[1024,16]{0,1:T(8,128)S(1)}, u32[]{:S(2)}) copy-start(f32[1024,16]{0,1:T(8,128)S(1)} %reshape.79) | copy-start | bytes 196612
  143.5 4.7 %copy-start.18 = (bf16[16,1024]{1,0:T(8,128)(2,1)S(1)}, bf16[16,1024]{1,0:T(8,128)(2,1)}, u32[]{:S(2)}) copy-start(bf16[16,1024]{1,0:T(8,128)(2,1)} %param.17) | copy-start | bytes 98308
  152.5 4.2 %copy-start.15 = (f32[16,48,16]{1,0,2:T(8,128)S(1)}, f32[16,48,16]{1,0,2:T(8,128)}, u32[]{:S(2)}) copy-start(f32[16,48,16]{1,0,2:T(8,128)} %copy-done.14) | copy-start | bytes 147460
  160.3 3.2 %copy-start.4 = (bf16[16,48,16]{2,0,1:T(8,128)(2,1)S(1)}, bf16[16,48,16]{2,0,1:T(8,128)(2,1)}, u32[]{:S(2)}) copy-start(bf16[16,48,16]{2,0,1:T(8,128)(2,1)} %copy.141) | copy-start | bytes 73732
  160.3 3.2 %copy-start.6 = (f32[1024,16]{0,1:T(8,128)S(1)}, f32[1024,16]{0,1:T(8,128)}, u32[]{:S(2)}) copy-start(f32[1024,16]{0,1:T(8,128)} %copy-done.5) | copy-start | bytes 196612
  160.3 5.5 %copy-start.8 = (bf16[16,48,16]{1,2,0:T(8,128)(2,1)S(1)}, bf16[16,48,16]{1,2,0:T(8,128)(2,1)}, u32[]{:S(2)}) copy-start(bf16[16,48,16]{1,2,0:T(8,128)(2,1)} %fusion.55) | copy-start | bytes 73732
  170.7 8.5 %copy-start.3 = (f32[48,16,1024]{2,1,0:T(8,128)S(1)}, f32[48,16,1024]{2,1,0:T(8,128)}, u32[]{:S(2)}) copy-start(f32[48,16,1024]{2,1,0:T(8,128)} %get-tuple-element.14) | copy-start | bytes 9437188
  170.7 8.5 %copy-start.11 = (f32[48,1024]{1,0:T(8,128)S(1)}, f32[48,1024]{1,0:T(8,128)}, u32[]{:S(2)}) copy-start(f32[48,1024]{1,0:T(8,128)} %copy-done.10) | copy-start | bytes 589828
  170.7 8.5 %copy-start.13 = (bf16[48,4,16]{2,1,0:T(4,128)(2,1)S(1)}, bf16[48,4,16]{2,1,0:T(4,128)(2,1)}, u32[]{:S(2)}) copy-start(bf16[48,4,16]{2,1,0:T(4,128)(2,1)} %copy-done.12) | copy-start | bytes 18436
  170.7 8.5 %copy-start.21 = (pred[48]{0:T(512)(128)(4,1)S(1)}, pred[48]{0:T(512)(128)(4,1)}, u32[]{:S(2)}) copy-start(pred[48]{0:T(512)(128)(4,1)} %copy-done.20) | copy-start | bytes 148
  182.8 3.5 %copy-start.19 = (pred[8,9]{1,0:T(8,128)(4,1)S(1)}, pred[8,9]{1,0:T(8,128)(4,1)}, u32[]{:S(2)}) copy-start(pred[8,9]{1,0:T(8,128)(4,1)} %broadcast_in_dim.69) | copy-start | bytes 220
  184.8 7.0 %copy-start.9 = (bf16[16,48,16]{1,2,0:T(8,128)(2,1)S(1)}, bf16[16,48,16]{1,2,0:T(8,128)(2,1)}, u32[]{:S(2)}) copy-start(bf16[16,48,16]{1,2,0:T(8,128)(2,1)} %fusion.55) | copy-start | bytes 73732
  187.6 21.6 %all-to-all-start.3 = ((f32[8,32,9,128]{3,1,2,0:T(8,128)}), f32[8,32,9,128]{3,1,2,0:T(8,128)}, u32[]{:S(2)}, u32[]{:S(2)}) async-start(f32[8,32,9,128]{3,1,2,0:T(8,128)} %select_bitcast_fusion), calls=%async_computation.3 | async-start | bytes 2359296 | tf_op jit(solution)/shard_map/all_to_all | solution.py:124
  211.3 18.1 %all-to-all-start.4 = ((f32[32,9,128]{2,1,0:T(8,128)}), f32[32,9,128]{2,1,0:T(8,128)S(1)}, u32[]{:S(2)}, u32[]{:S(2)}) async-start(f32[32,9,128]{2,1,0:T(8,128)} %copy.144), calls=%async_computation.4 | async-start | bytes 524288 | tf_op jit(solution)/shard_map/all_to_all | solution.py:125
  (4 other events, 6.8 us)
